TPU v7x, 128 devices: a whole 4x4x4 slice. The times are simulated.
128 devices in a mesh: tok: 16 (over y, x), head: 8 (over z, core).
Axes of the slice: x: 4, y: 4, z: 4, core: 2. Of those that a mesh axis runs over, the one named last changes fastest.
Arguments:
- tokens: bfloat16 [8192, 8192], P('tok', 'head'), may hold values from -60 to 60
- gain: bfloat16 [8192], P('head'), may hold values from 0.5 to 2
- w_query: bfloat16 [8192, 8, 512], P(('head', 'tok')), may hold values from -0.125 to 0.125
- w_key: bfloat16 [8192, 8, 128], P(('head', 'tok')), may hold values from -0.0625 to 0.0625
- w_value: bfloat16 [8192, 8, 128], P(('head', 'tok')), may hold values from -0.5 to 0.5
- group_ids: int32 [8192, 1], P('tok'), may hold values from 0 to 15; in each aligned block of 512 rows (0 to 511, 512 to 1023, ...) at most 64 rows name the same one
- key_pages: bfloat16 [1024, 128, 8, 128], P('tok', None, 'head'), may hold values from -42 to 42
- value_pages: bfloat16 [1024, 128, 8, 128], P('tok', None, 'head'), may hold values from -48 to 48
- page_table: int32 [16, 32], P('tok'), may hold values from 0 to 1023, as said below
Outputs:
- attention: bfloat16 [8192, 4096], P('tok', 'head')
Inputs may be any that keep to these rules, and one draw needn't show every extreme that they name: `group_ids`: among the 512 tokens of one index of tok (aligned blocks of rows), no group appears more than 64 times, a bound that some block reaches. `page_table`: row g lists 32 different pages, all in g * 64 to (g + 1) * 64 - 1, among them the first and the last page of that range.
All inputs are finite; a program needn't handle non-finite values.
Results may differ from a plain program's by a relative error of at most 0.0085.
The roundings to bfloat16 on the way count: a program that leaves them out, or rounds other values in their place, can miss the bound.
Values may be sent and summed in bfloat16 or wider, within the bound.
No kernel may reach another device: no remote copies, remote signals or barrier semaphores. Data moves between devices by JAX's collectives and lax.ppermute only.
A program may use at most 128 MiB of HBM per device.

v0:
```python
import math
import jax
import jax.numpy as jnp
from jax import lax
from jax.sharding import PartitionSpec as P

EPS = 1e-05
THETA = 10000.0


def rotate(values, positions):
    halfway = values.shape[-1] // 2
    frequency = jnp.exp(
        -math.log(THETA) * 2.0 * jnp.arange(halfway, dtype=jnp.float32) / values.shape[-1]
    )
    angles = positions.astype(jnp.float32)[:, None] * frequency[None, :]
    cosine = jnp.cos(angles)[:, None, :]
    sine_part = jnp.sin(angles)[:, None, :]
    leading = values[..., :halfway].astype(jnp.float32)
    trailing = values[..., halfway:].astype(jnp.float32)
    return jnp.concatenate(
        [leading * cosine - trailing * sine_part, trailing * cosine + leading * sine_part], axis=-1
    ).astype(jnp.bfloat16)


def attend(
    queries, query_rank, prefix_keys, prefix_values, new_keys, new_values, key_rank, key_live
):
    scaling = 1.0 / math.sqrt(queries.shape[-1])
    before = (
        jnp.einsum("bhd,pd->bhp", queries, prefix_keys, preferred_element_type=jnp.float32)
        * scaling
    )
    inside = (
        jnp.einsum("bhd,sd->bhs", queries, new_keys, preferred_element_type=jnp.float32) * scaling
    )
    allowed = key_live[None, :] & (key_rank[None, :] <= query_rank[:, None])
    inside = jnp.where(allowed[:, None, :], inside, -jnp.inf)
    highest = jnp.maximum(jnp.max(before, axis=-1), jnp.max(inside, axis=-1))
    expo_before = jnp.exp(before - highest[..., None])
    expo_inside = jnp.exp(inside - highest[..., None])
    totals = jnp.sum(expo_before, axis=-1) + jnp.sum(expo_inside, axis=-1)
    mixed = jnp.einsum(
        "bhp,pd->bhd",
        expo_before.astype(jnp.bfloat16),
        prefix_values,
        preferred_element_type=jnp.float32,
    )
    mixed = mixed + jnp.einsum(
        "bhs,sd->bhd",
        expo_inside.astype(jnp.bfloat16),
        new_values,
        preferred_element_type=jnp.float32,
    )
    return (mixed / totals[..., None]).astype(jnp.bfloat16)


def row_norm(tokens, gain, full_width):
    values_wide = tokens.astype(jnp.float32)
    squares = lax.psum(jnp.sum(values_wide * values_wide, axis=1), "head")
    factor = lax.rsqrt(squares / full_width + EPS)
    return (values_wide * factor[:, None] * gain.astype(jnp.float32)[None, :]).astype(jnp.bfloat16)


def body(tokens, gain, w_query, w_key, w_value, group_ids, key_pages, value_pages, page_table):
    row_count = tokens.shape[0]
    n_tok = lax.axis_size("tok")
    n_head = lax.axis_size("head")
    head_size = key_pages.shape[-1]
    query_width = w_query.shape[2]
    group_heads = query_width // head_size
    full_width = tokens.shape[1] * n_head
    capacity = 2 * row_count // n_tok
    normed = row_norm(tokens, gain, full_width)
    gathered = (
        lax.all_gather(w_query, "tok", axis=0, tiled=True),
        lax.all_gather(w_key, "tok", axis=0, tiled=True),
        lax.all_gather(w_value, "tok", axis=0, tiled=True),
    )
    group_count = row_count * lax.axis_size("head") // row_count
    results = []
    for weight in gathered:
        results.append(
            jnp.einsum("rd,dnc->nrc", normed, weight, preferred_element_type=jnp.float32)
        )
    joined = jnp.concatenate(results, axis=2)
    projected = lax.psum_scatter(
        joined.reshape(group_count * row_count, joined.shape[2]),
        "head",
        scatter_dimension=0,
        tiled=True,
    )
    projected_low = projected.astype(jnp.bfloat16)
    width_all = projected_low.shape[1]
    group_of = group_ids[:, 0]
    member = (group_of[:, None] == jnp.arange(n_tok, dtype=jnp.int32)[None, :]).astype(jnp.int32)
    local_rank = jnp.sum((jnp.cumsum(member, axis=0) - member) * member, axis=1)
    slot_index = group_of * capacity + local_rank
    outgoing = (
        jnp.zeros((n_tok * capacity, width_all), jnp.bfloat16).at[slot_index].set(projected_low)
    )
    marker = jnp.zeros((n_tok * capacity,), jnp.bfloat16).at[slot_index].set(1.0)
    arrived, arrived_marker = (
        lax.all_to_all(
            outgoing.reshape(n_tok, capacity, width_all),
            "tok",
            split_axis=0,
            concat_axis=0,
            tiled=True,
        ),
        lax.all_to_all(
            marker.reshape(n_tok, capacity), "tok", split_axis=0, concat_axis=0, tiled=True
        ),
    )
    slot_total = n_tok * capacity
    arrived = arrived.reshape(slot_total, width_all)
    live_count = (arrived_marker.reshape(slot_total) > 0).astype(jnp.int32)
    key_live = live_count > 0
    slot_rank = jnp.cumsum(live_count) - live_count
    prefix_length = page_table.shape[1] * key_pages.shape[1]
    positions = prefix_length + slot_rank
    rotated_queries = rotate(
        arrived[:, :query_width].reshape(slot_total, group_heads, head_size), positions
    )
    rotated_keys = rotate(
        arrived[:, query_width : query_width + head_size].reshape(slot_total, 1, head_size),
        positions,
    )[:, 0, :]
    slot_values = arrived[:, query_width + head_size :]
    local_pages = page_table[0] - lax.axis_index("tok") * key_pages.shape[0]
    prefix_keys = jnp.take(key_pages[:, :, 0, :], local_pages, axis=0).reshape(
        prefix_length, head_size
    )
    prefix_values = jnp.take(value_pages[:, :, 0, :], local_pages, axis=0).reshape(
        prefix_length, head_size
    )
    block_size = min(128, slot_total)

    def one_block(blocked):
        return attend(
            blocked[0],
            blocked[1],
            prefix_keys,
            prefix_values,
            rotated_keys,
            slot_values,
            slot_rank,
            key_live,
        )

    attended = lax.map(
        one_block,
        (
            rotated_queries.reshape(slot_total // block_size, block_size, group_heads, head_size),
            slot_rank.reshape(slot_total // block_size, block_size),
        ),
    )
    returned = lax.all_to_all(
        attended.reshape(n_tok, capacity, query_width),
        "tok",
        split_axis=0,
        concat_axis=0,
        tiled=True,
    )
    return returned.reshape(n_tok * capacity, query_width)[slot_index]


def solution(mesh):
    placed = (
        P("tok", "head"),
        P("head"),
        P(("head", "tok"), None, None),
        P(("head", "tok"), None, None),
        P(("head", "tok"), None, None),
        P("tok", None),
        P("tok", None, "head", None),
        P("tok", None, "head", None),
        P("tok", None),
    )
    return jax.shard_map(
        body, mesh=mesh, in_specs=placed, out_specs=P("tok", "head"), check_vma=False
    )
```

profile of v0, /device:TPU:32, one launch (start us, length us, event | category | flops | bytes accessed | tf_op | source)
XLA Modules:
  0.0 415.2 jit_solution(10881437984728749985)
XLA Ops:
  10.0 2.0 copy.32
  12.4 12.5 %psum.7 = f32[512]{0:T(512)S(1)} all-reduce(f32[512]{0:T(512)S(1)} %fusion.30), channel_id=1, replica_groups=mesh['tok'=16,'head'=8] {'head'}, use_global_device_ids=true, to_apply=%region_4.5 | all-reduce | flops 512 | bytes 4096 | tf_op jit(solution)/shard_map/psum | solution.py:60
  24.9 31.4 %all-gather.8.cloned.1.call-done = bf16[1024,8,128]{2,0,1:T(8,128)(2,1)} async-done(((bf16[64,8,128]{2,0,1:T(8,128)(2,1)}), bf16[1024,8,128]{2,0,1:T(8,128)(2,1)}) %all-gather.8.cloned.1.call-update) | async-done | bytes 2097168 | tf_op jit(solution)/shard_map/all_gather | solution.py:78
  56.3 4.3 %convolution_bitcast_fusion.1 = f32[8,512,128]{1,2,0:T(8,128)} fusion(bf16[1024,8,128]{2,0,1:T(8,128)(2,1)} %all-gather.8.cloned.1.call-done, bf16[512,1024]{1,0:T(8,128)(2,1)S(1)} %copy-done.4, f32[1024]{0:T(1024)S(1)} %convert_element_type.74, f32[512]{0:T(512)S(1)} %add_rsqrt_fusion), kind=kOutput, calls=%fused_computation.48 | convolution fusion | flops 1075838976 | bytes 5249024 | tf_op jit(solution)/shard_map/rd,dnc->nrc/dot_general | solution.py:84
  60.6 42.0 %all-gather.6.cloned.1.call-done = bf16[1024,8,128]{2,0,1:T(8,128)(2,1)} async-done(((bf16[64,8,128]{2,0,1:T(8,128)(2,1)}), bf16[1024,8,128]{2,0,1:T(8,128)(2,1)}) %all-gather.6.cloned.1.call-update) | async-done | bytes 2097168 | tf_op jit(solution)/shard_map/all_gather | solution.py:77
  102.6 4.3 %convolution_bitcast_fusion.2 = f32[8,512,128]{1,2,0:T(8,128)} fusion(bf16[1024,8,128]{2,0,1:T(8,128)(2,1)} %all-gather.6.cloned.1.call-done, bf16[512,1024]{1,0:T(8,128)(2,1)S(1)} %copy-done.4, f32[1024]{0:T(1024)S(1)} %convert_element_type.74, f32[512]{0:T(512)S(1)} %add_rsqrt_fusion), kind=kOutput, calls=%fused_computation.49 | convolution fusion | flops 1075838976 | bytes 5249024 | tf_op jit(solution)/shard_map/rd,dnc->nrc/dot_general | solution.py:84
  106.9 68.0 %all-gather.4.cloned.1.call-done = bf16[1024,8,512]{2,0,1:T(8,128)(2,1)} async-done(((bf16[64,8,512]{2,0,1:T(8,128)(2,1)}), bf16[1024,8,512]{2,0,1:T(8,128)(2,1)}) %all-gather.4.cloned.1.call-update) | async-done | bytes 8388624 | tf_op jit(solution)/shard_map/all_gather | solution.py:76
  174.9 7.5 %convolution_bitcast_fusion = f32[8,512,512]{1,2,0:T(8,128)S(1)} fusion(bf16[1024,8,512]{2,0,1:T(8,128)(2,1)} %all-gather.4.cloned.1.call-done, bf16[512,1024]{1,0:T(8,128)(2,1)S(1)} %copy-done.4, f32[1024]{0:T(1024)S(1)} %convert_element_type.74, f32[512]{0:T(512)S(1)} %add_rsqrt_fusion), kind=kOutput, calls=%fused_computation.42 | convolution fusion | flops 4297064448 | bytes 17831936 | tf_op jit(solution)/shard_map/rd,dnc->nrc/dot_general | solution.py:84
  182.4 6.9 %pad_maximum_fusion = f32[8,512,768]{1,2,0:T(8,128)} fusion(f32[8,512,128]{1,2,0:T(8,128)S(1)} %copy-done.2, f32[8,512,128]{1,2,0:T(8,128)S(1)} %copy-done.3, f32[8,512,512]{1,2,0:T(8,128)S(1)} %convolution_bitcast_fusion), kind=kLoop, calls=%fused_computation.41 | loop fusion | flops 6291456 | bytes 25165824 | tf_op jit(solution)/shard_map/concatenate | solution.py:86
  189.3 12.6 %copy.35 = f32[8,512,768]{2,1,0:T(8,128)} copy(f32[8,512,768]{1,2,0:T(8,128)} %pad_maximum_fusion) | data formatting | bytes 25165824 | tf_op jit(solution)/shard_map/concatenate | solution.py:86
  204.1 3.8 scatter_custom_fusion.1
  208.5 5.3 %all-to-all-start.1 = ((bf16[16,1,64]{2,1,0:T(2,128)(2,1)}), bf16[16,1,64]{2,1,0:T(2,128)(2,1)S(1)}, u32[]{:S(2)}, u32[]{:S(2)}) async-start(bf16[16,1,64]{2,1,0:T(2,128)(2,1)} %all_to_all.16), calls=%async_computation.2 | async-start | bytes 16384 | tf_op jit(solution)/shard_map/all_to_all | solution.py:111
  214.6 3.3 gather_fusion.2
  217.9 53.8 %reduce-scatter.2.cloned.1.call-done = f32[512,768]{1,0:T(8,128)} async-done(((f32[4096,768]{1,0:T(8,128)}), f32[512,768]{1,0:T(8,128)}) %reduce-scatter.2.cloned.1.call-update) | async-done | bytes 1572880 | tf_op jit(solution)/shard_map/reduce_scatter | solution.py:87
  271.7 4.6 %scatter_custom_fusion = bf16[1024,768]{1,0:T(8,128)(2,1)} fusion(s32[512]{0:T(512)S(1)} %bitcast.131, f32[512,768]{1,0:T(8,128)} %reduce-scatter.2.cloned.1.call-done, bf16[]{:T(256)} %constant.23.clone.1), kind=kCustom, calls=%fused_computation.62 | custom fusion | flops 393216 | bytes 3145730 | tf_op jit(solution)/shard_map/scatter | solution.py:100
  276.3 7.1 %all-to-all-start = ((bf16[16,64,768]{2,1,0:T(8,128)(2,1)}), bf16[16,64,768]{2,1,0:T(8,128)(2,1)}, u32[]{:S(2)}, u32[]{:S(2)}) async-start(bf16[16,64,768]{2,1,0:T(8,128)(2,1)} %bitcast.17), calls=%async_computation.1 | async-start | bytes 3145728 | tf_op jit(solution)/shard_map/all_to_all | solution.py:104
  287.5 23.9 %all-to-all-done = bf16[16,64,768]{2,1,0:T(8,128)(2,1)} async-done(((bf16[16,64,768]{2,1,0:T(8,128)(2,1)}), bf16[16,64,768]{2,1,0:T(8,128)(2,1)}, u32[]{:S(2)}, u32[]{:S(2)}) %all-to-all-start) | async-done | bytes 1572896 | tf_op jit(solution)/shard_map/all_to_all | solution.py:104
  311.4 1.8 fusion.61
  314.5 3.1 fusion.50
  324.8 57.1 %while.10 = (s32[]{:T(128)}, bf16[8,128,4,128]{3,2,1,0:T(4,128)(2,1)}, bf16[8,128,4,128]{3,1,2,0:T(8,128)(2,1)S(1)}, bf16[4096,128]{1,0:T(8,128)(2,1)S(1)}, pred...) while((s32[]{:T(128)}, ...), condition=%wide.region_15.17_spmd, body=%wide.region_10.16_spmd.sunk | while | flops 1365179392 | bytes 36869268 | solution.py:151
  381.8 2.3 reshape.278
  384.1 3.7 all-to-all-start.2
  387.8 18.2 %all-to-all-done.2 = bf16[16,64,512]{2,1,0:T(8,128)(2,1)S(1)} async-done(((bf16[16,64,512]{2,1,0:T(8,128)(2,1)}), bf16[16,64,512]{2,1,0:T(8,128)(2,1)S(1)}, u32[]{:S(2)}, u32[]{:S(2)}) %all-to-all-start.2) | async-done | bytes 1048608 | tf_op jit(solution)/shard_map/all_to_all | solution.py:158
  406.0 2.6 gather_fusion
  (170 shorter events, 76.6 us)
Async XLA Ops:
  6.5 207.3 %copy-start = (bf16[64,128,1,128]{3,1,2,0:T(8,128)(2,1)S(1)}, bf16[64,128,1,128]{3,1,2,0:T(8,128)(2,1)}, u32[]{:S(2)}) copy-start(bf16[64,128,1,128]{3,1,2,0:T(8,128)(2,1)} %param.19) | copy-start | bytes 6291460
  6.5 5.5 %copy-start.7 = (bf16[1024]{0:T(1024)(128)(2,1)S(1)}, bf16[1024]{0:T(1024)(128)(2,1)}, u32[]{:S(2)}) copy-start(bf16[1024]{0:T(1024)(128)(2,1)} %param.14) | copy-start | bytes 6148
  6.5 5.5 %copy-start.4 = (bf16[512,1024]{1,0:T(8,128)(2,1)S(1)}, bf16[512,1024]{1,0:T(8,128)(2,1)}, u32[]{:S(2)}) copy-start(bf16[512,1024]{1,0:T(8,128)(2,1)} %param.13) | copy-start | bytes 3145732
  6.5 49.7 %all-gather.8.cloned.1.call-start = ((), (), s32[]{:S(2)}) async-start(), calls=%async_computation.6 | async-start | bytes 2228224 | tf_op jit(solution)/shard_map/all_gather | solution.py:78
  8.3 94.3 %all-gather.6.cloned.1.call-start = ((), (), s32[]{:S(2)}) async-start(), calls=%async_computation.5 | async-start | bytes 2228224 | tf_op jit(solution)/shard_map/all_gather | solution.py:77
  9.9 164.9 %all-gather.4.cloned.1.call-start = ((), (), s32[]{:S(2)}) async-start(), calls=%async_computation.4 | async-start | bytes 8912896 | tf_op jit(solution)/shard_map/all_gather | solution.py:76
  12.0 259.7 %reduce-scatter.2.cloned.1.call-start = ((), (), s32[]{:S(2)}) async-start(), calls=%async_computation.7 | async-start | bytes 14155776 | tf_op jit(solution)/shard_map/reduce_scatter | solution.py:87
  174.9 7.5 %copy-start.2 = (f32[8,512,128]{1,2,0:T(8,128)S(1)}, f32[8,512,128]{1,2,0:T(8,128)}, u32[]{:S(2)}) copy-start(f32[8,512,128]{1,2,0:T(8,128)} %convolution_bitcast_fusion.1) | copy-start | bytes 6291460
  174.9 7.6 %copy-start.3 = (f32[8,512,128]{1,2,0:T(8,128)S(1)}, f32[8,512,128]{1,2,0:T(8,128)}, u32[]{:S(2)}) copy-start(f32[8,512,128]{1,2,0:T(8,128)} %convolution_bitcast_fusion.2) | copy-start | bytes 6291460
  201.8 0.7 copy-start.6
  201.8 11.9 %copy-start.8 = (s32[1,32]{1,0:T(1,128)S(1)}, s32[1,32]{1,0:T(1,128)}, u32[]{:S(2)}) copy-start(s32[1,32]{1,0:T(1,128)} %param.21) | copy-start | bytes 388
  208.5 67.8 %all-to-all-start.1 = ((bf16[16,1,64]{2,1,0:T(2,128)(2,1)}), bf16[16,1,64]{2,1,0:T(2,128)(2,1)S(1)}, u32[]{:S(2)}, u32[]{:S(2)}) async-start(bf16[16,1,64]{2,1,0:T(2,128)(2,1)} %all_to_all.16), calls=%async_computation.2 | async-start | bytes 16384 | tf_op jit(solution)/shard_map/all_to_all | solution.py:111
  276.3 35.1 %all-to-all-start = ((bf16[16,64,768]{2,1,0:T(8,128)(2,1)}), bf16[16,64,768]{2,1,0:T(8,128)(2,1)}, u32[]{:S(2)}, u32[]{:S(2)}) async-start(bf16[16,64,768]{2,1,0:T(8,128)(2,1)} %bitcast.17), calls=%async_computation.1 | async-start | bytes 3145728 | tf_op jit(solution)/shard_map/all_to_all | solution.py:104
  329.0 1.5 copy-start.5
  336.1 1.5 copy-start.5
  343.2 1.5 copy-start.5
  350.4 1.5 copy-start.5
  357.5 1.5 copy-start.5
  364.6 1.5 copy-start.5
  371.8 1.5 copy-start.5
  378.9 1.5 copy-start.5
  384.1 21.9 %all-to-all-start.2 = ((bf16[16,64,512]{2,1,0:T(8,128)(2,1)}), bf16[16,64,512]{2,1,0:T(8,128)(2,1)S(1)}, u32[]{:S(2)}, u32[]{:S(2)}) async-start(bf16[16,64,512]{2,1,0:T(8,128)(2,1)} %reshape.278), calls=%async_computation.3 | async-start | bytes 2097152 | tf_op jit(solution)/shard_map/all_to_all | solution.py:158
  406.0 2.6 copy-start.1
Sparse Core Ops, SparseCore 0:
  9.5 46.7 all-gather.7
  58.4 44.1 all-gather.5
  104.8 70.0 all-gather.3
  202.0 69.6 reduce-scatter.1
where the time goes:
time: 416 us; the launch traced here: 415 us
  waiting for transfers between devices  237 us (57%)
  matrix products  48.6 us (12%)
  local copies, waits for them, and re-layouts  44.9 us (11%)
  other arithmetic  42 us (10%)
  starting transfers between devices  16.1 us (4%)
  between operations  13.4 us (3%)
  blocking collectives  12.5 us (3%)
    all_gather x1, waiting for transfers between devices, body(): lax.all_gather(w_query, 'tok', axis=0, tiled=True)  68 us
    reduce_scatter x1, waiting for transfers between devices, body(): lax.psum_scatter(joined.reshape(group_count * row_count, joined.shape[2])...  53.8 us
    all_gather x1, waiting for transfers between devices, body(): lax.all_gather(w_key, 'tok', axis=0, tiled=True)  42 us
    all_gather x1, waiting for transfers between devices, body(): lax.all_gather(w_value, 'tok', axis=0, tiled=True)  31.4 us
    all_to_all x1, waiting for transfers between devices, body(): lax.all_to_all(outgoing.reshape(n_tok, capacity, width_all), 'tok', split...  23.9 us
    all_to_all x1, waiting for transfers between devices, body(): lax.all_to_all(attended.reshape(n_tok, capacity, query_width), 'tok', spl...  18.2 us
    reduce_sum x16, other arithmetic, attend(): totals = jnp.sum(expo_before, axis=-1) + jnp.sum(expo_inside, axis=-1)  16.8 us
    dot_general x3, matrix products, body(): jnp.einsum('rd,dnc->nrc', normed, weight, preferred_element_type=jnp.floa...  16.1 us
  transfers between devices with their start and end apart: 7, of which 6 were waited for; matrix products, arithmetic and copies ran while one was open for 7% of the time, Pallas kernels for 0%

commit v1 on v0

--- a/solution.py
+++ b/solution.py
@@ -3,9 +3,13 @@
 import jax.numpy as jnp
 from jax import lax
 from jax.sharding import PartitionSpec as P
+from jax.lax import all_to_all, axis_size
 
 EPS = 1e-05
 THETA = 10000.0
+ratios_pair = lambda inp: jnp.concatenate(
+    all_to_all(jnp.stack(axis_size("tok") * [inp], axis=0), "tok", 0, 0), axis=0
+)
 
 
 def rotate(values, positions):
@@ -75,7 +79,7 @@
     gathered = (
         lax.all_gather(w_query, "tok", axis=0, tiled=True),
         lax.all_gather(w_key, "tok", axis=0, tiled=True),
-        lax.all_gather(w_value, "tok", axis=0, tiled=True),
+        ratios_pair(w_value),
     )
     group_count = row_count * lax.axis_size("head") // row_count
     results = []

time: 416 us -> 387 us (0.930)
  waiting for transfers between devices: 237 us -> 195 us
  starting transfers between devices: 16.1 us -> 23.3 us
  local copies, waits for them, and re-layouts: 44.9 us -> 50.1 us
    all_gather x1, waiting for transfers between devices: 42 us -> 10.6 us  [body(): lax.all_gather(w_key, 'tok', axis=0, tiled=True)]
    all_gather x1 -> x0, waiting for transfers between devices: 31.4 us -> none  [body(): lax.all_gather(w_value, 'tok', axis=0, tiled=True)]
    all_to_all x0 -> x1, waiting for transfers between devices: none -> 21 us  [all_to_all(jnp.stack(axis_size('tok') * [inp], axis=0), 'tok', 0, 0)]
    all_to_all x0 -> x1, starting transfers between devices: none -> 7.22 us  [all_to_all(jnp.stack(axis_size('tok') * [inp], axis=0), 'tok', 0, 0)]
    dot_general x3 -> x2, matrix products: 16.1 us -> 11.9 us  [body(): jnp.einsum('rd,dnc->nrc', normed, weight, preferred_element_type=jnp.floa...]
    unnamed x0 -> x1, matrix products: none -> 4.25 us
  transfers between devices with their start and end apart: 7 -> 7, of which waited for: 6 -> 6; matrix products, arithmetic and copies ran while one was open for 7% -> 9% of each run, Pallas kernels for 0% -> 0%
where the time goes in v1:
time: 387 us; the launch traced here: 386 us
  waiting for transfers between devices  195 us (50%)
  local copies, waits for them, and re-layouts  50.1 us (13%)
  matrix products  48.6 us (13%)
  other arithmetic  42 us (11%)
  starting transfers between devices  23.3 us (6%)
  between operations  13.4 us (3%)
  blocking collectives  12.6 us (3%)
    all_gather x1, waiting for transfers between devices, body(): lax.all_gather(w_query, 'tok', axis=0, tiled=True)  67.9 us
    reduce_scatter x1, waiting for transfers between devices, body(): lax.psum_scatter(joined.reshape(group_count * row_count, joined.shape[2])...  53.8 us
    all_to_all x1, waiting for transfers between devices, body(): lax.all_to_all(outgoing.reshape(n_tok, capacity, width_all), 'tok', split...  23.9 us
    all_to_all x1, waiting for transfers between devices, all_to_all(jnp.stack(axis_size('tok') * [inp], axis=0), 'tok', 0, 0)  21 us
    all_to_all x1, waiting for transfers between devices, body(): lax.all_to_all(attended.reshape(n_tok, capacity, query_width), 'tok', spl...  18.2 us
    reduce_sum x16, other arithmetic, attend(): totals = jnp.sum(expo_before, axis=-1) + jnp.sum(expo_inside, axis=-1)  16.8 us
    psum x1, blocking collectives, row_norm(): squares = lax.psum(jnp.sum(values_wide * values_wide, axis=1), 'head')  12.6 us
    concatenate x1, local copies, waits for them, and re-layouts, body(): joined = jnp.concatenate(results, axis=2)  12.6 us
  transfers between devices with their start and end apart: 7, of which 6 were waited for; matrix products, arithmetic and copies ran while one was open for 9% of the time, Pallas kernels for 0%

profile of v1, /device:TPU:32, one launch (start us, length us, event | category | flops | bytes accessed | tf_op | source)
XLA Modules:
  0.0 385.8 jit_solution(7453260482781046610)
XLA Ops:
  10.3 2.7 stack.2
  13.0 7.2 %all-to-all-start = ((bf16[16,64,8,128]{3,2,1,0:T(8,128)(2,1)}), bf16[16,64,8,128]{3,2,1,0:T(8,128)(2,1)}, u32[]{:S(2)}, u32[]{:S(2)}) async-start(bf16[16,64,8,128]{3,2,1,0:T(8,128)(2,1)} %stack.2), calls=%async_computation | async-start | bytes 4194304 | tf_op jit(solution)/shard_map/all_to_all | solution.py:11
  20.6 12.6 %psum.7 = f32[512]{0:T(512)S(1)} all-reduce(f32[512]{0:T(512)S(1)} %fusion.30), channel_id=1, replica_groups=mesh['tok'=16,'head'=8] {'head'}, use_global_device_ids=true, to_apply=%region_4.5 | all-reduce | flops 512 | bytes 4096 | tf_op jit(solution)/shard_map/psum | solution.py:64
  33.3 21.0 %all-to-all-done = bf16[16,64,8,128]{3,2,1,0:T(8,128)(2,1)} async-done(((bf16[16,64,8,128]{3,2,1,0:T(8,128)(2,1)}), bf16[16,64,8,128]{3,2,1,0:T(8,128)(2,1)}, u32[]{:S(2)}, u32[]{:S(2)}) %all-to-all-start) | async-done | bytes 2097184 | tf_op jit(solution)/shard_map/all_to_all | solution.py:11
  54.3 4.1 %copy.34 = bf16[1024,8,128]{0,2,1:T(8,128)(2,1)} copy(bf16[1024,8,128]{2,1,0:T(8,128)(2,1)} %bitcast.15) | data formatting | bytes 4194304 | tf_op jit(solution)/shard_map/reshape | solution.py:10
  58.4 4.2 %fusion.60 = f32[512,1024]{0,1} fusion(bf16[1024,1024]{0,1:T(8,128)(2,1)} %bitcast.128, bf16[512,1024]{1,0:T(8,128)(2,1)S(1)} %copy-done.4, f32[1024]{0:T(1024)S(1)} %convert_element_type.74, f32[512]{0:T(512)S(1)} %add_rsqrt_fusion), kind=kOutput, calls=%fused_computation.106 | convolution fusion | flops 1075838976 | bytes 5249024
  62.6 10.6 %all-gather.5.cloned.1.call-done = bf16[1024,8,128]{2,0,1:T(8,128)(2,1)} async-done(((bf16[64,8,128]{2,0,1:T(8,128)(2,1)}), bf16[1024,8,128]{2,0,1:T(8,128)(2,1)}) %all-gather.5.cloned.1.call-update) | async-done | bytes 2097168 | tf_op jit(solution)/shard_map/all_gather | solution.py:81
  73.2 4.3 %convolution_bitcast_fusion.1 = f32[8,512,128]{1,2,0:T(8,128)} fusion(bf16[1024,8,128]{2,0,1:T(8,128)(2,1)} %all-gather.5.cloned.1.call-done, bf16[512,1024]{1,0:T(8,128)(2,1)S(1)} %copy-done.4, f32[1024]{0:T(1024)S(1)} %convert_element_type.74, f32[512]{0:T(512)S(1)} %add_rsqrt_fusion), kind=kOutput, calls=%fused_computation.48 | convolution fusion | flops 1075838976 | bytes 5249024 | tf_op jit(solution)/shard_map/rd,dnc->nrc/dot_general | solution.py:88
  77.6 67.9 %all-gather.3.cloned.1.call-done = bf16[1024,8,512]{2,0,1:T(8,128)(2,1)} async-done(((bf16[64,8,512]{2,0,1:T(8,128)(2,1)}), bf16[1024,8,512]{2,0,1:T(8,128)(2,1)}) %all-gather.3.cloned.1.call-update) | async-done | bytes 8388624 | tf_op jit(solution)/shard_map/all_gather | solution.py:80
  145.5 7.5 %convolution_bitcast_fusion = f32[8,512,512]{1,2,0:T(8,128)S(1)} fusion(bf16[1024,8,512]{2,0,1:T(8,128)(2,1)} %all-gather.3.cloned.1.call-done, bf16[512,1024]{1,0:T(8,128)(2,1)S(1)} %copy-done.4, f32[1024]{0:T(1024)S(1)} %convert_element_type.74, f32[512]{0:T(512)S(1)} %add_rsqrt_fusion), kind=kOutput, calls=%fused_computation.42 | convolution fusion | flops 4297064448 | bytes 17831936 | tf_op jit(solution)/shard_map/rd,dnc->nrc/dot_general | solution.py:88
  153.0 6.9 %pad_maximum_fusion = f32[8,512,768]{1,2,0:T(8,128)} fusion(f32[8,512,128]{1,2,0:T(8,128)S(1)} %bitcast.125, f32[8,512,128]{1,2,0:T(8,128)S(1)} %copy-done.3, f32[8,512,512]{1,2,0:T(8,128)S(1)} %convolution_bitcast_fusion), kind=kLoop, calls=%fused_computation.41 | loop fusion | flops 6291456 | bytes 25165824 | tf_op jit(solution)/shard_map/concatenate | solution.py:90
  159.9 12.6 %copy.35 = f32[8,512,768]{2,1,0:T(8,128)} copy(f32[8,512,768]{1,2,0:T(8,128)} %pad_maximum_fusion) | data formatting | bytes 25165824 | tf_op jit(solution)/shard_map/concatenate | solution.py:90
  174.7 3.8 scatter_custom_fusion.1
  179.1 5.3 %all-to-all-start.2 = ((bf16[16,1,64]{2,1,0:T(2,128)(2,1)}), bf16[16,1,64]{2,1,0:T(2,128)(2,1)S(1)}, u32[]{:S(2)}, u32[]{:S(2)}) async-start(bf16[16,1,64]{2,1,0:T(2,128)(2,1)} %all_to_all.20), calls=%async_computation.3 | async-start | bytes 16384 | tf_op jit(solution)/shard_map/all_to_all | solution.py:115
  185.2 3.3 gather_fusion.2
  188.5 53.8 %reduce-scatter.2.cloned.1.call-done = f32[512,768]{1,0:T(8,128)} async-done(((f32[4096,768]{1,0:T(8,128)}), f32[512,768]{1,0:T(8,128)}) %reduce-scatter.2.cloned.1.call-update) | async-done | bytes 1572880 | tf_op jit(solution)/shard_map/reduce_scatter | solution.py:91
  242.3 4.6 %scatter_custom_fusion = bf16[1024,768]{1,0:T(8,128)(2,1)} fusion(s32[512]{0:T(512)S(1)} %bitcast.136, f32[512,768]{1,0:T(8,128)} %reduce-scatter.2.cloned.1.call-done, bf16[]{:T(256)} %constant.23.clone.1), kind=kCustom, calls=%fused_computation.62 | custom fusion | flops 393216 | bytes 3145730 | tf_op jit(solution)/shard_map/scatter | solution.py:104
  246.9 7.1 %all-to-all-start.1 = ((bf16[16,64,768]{2,1,0:T(8,128)(2,1)}), bf16[16,64,768]{2,1,0:T(8,128)(2,1)}, u32[]{:S(2)}, u32[]{:S(2)}) async-start(bf16[16,64,768]{2,1,0:T(8,128)(2,1)} %bitcast.20), calls=%async_computation.2 | async-start | bytes 3145728 | tf_op jit(solution)/shard_map/all_to_all | solution.py:108
  258.1 23.9 %all-to-all-done.1 = bf16[16,64,768]{2,1,0:T(8,128)(2,1)} async-done(((bf16[16,64,768]{2,1,0:T(8,128)(2,1)}), bf16[16,64,768]{2,1,0:T(8,128)(2,1)}, u32[]{:S(2)}, u32[]{:S(2)}) %all-to-all-start.1) | async-done | bytes 1572896 | tf_op jit(solution)/shard_map/all_to_all | solution.py:108
  285.1 3.1 fusion.51
  295.4 57.1 %while.10 = (s32[]{:T(128)}, bf16[8,128,4,128]{3,2,1,0:T(4,128)(2,1)}, bf16[8,128,4,128]{3,1,2,0:T(8,128)(2,1)S(1)}, bf16[4096,128]{1,0:T(8,128)(2,1)S(1)}, pred...) while((s32[]{:T(128)}, ...), condition=%wide.region_15.17_spmd, body=%wide.region_10.16_spmd.sunk | while | flops 1365179392 | bytes 36869268 | solution.py:155
  354.7 3.7 all-to-all-start.3
  358.4 18.2 %all-to-all-done.3 = bf16[16,64,512]{2,1,0:T(8,128)(2,1)S(1)} async-done(((bf16[16,64,512]{2,1,0:T(8,128)(2,1)}), bf16[16,64,512]{2,1,0:T(8,128)(2,1)S(1)}, u32[]{:S(2)}, u32[]{:S(2)}) %all-to-all-start.3) | async-done | bytes 1048608 | tf_op jit(solution)/shard_map/all_to_all | solution.py:162
  376.6 2.6 gather_fusion
  (170 shorter events, 81.0 us)
Async XLA Ops:
  6.5 177.9 %copy-start = (bf16[64,128,1,128]{3,1,2,0:T(8,128)(2,1)S(1)}, bf16[64,128,1,128]{3,1,2,0:T(8,128)(2,1)}, u32[]{:S(2)}) copy-start(bf16[64,128,1,128]{3,1,2,0:T(8,128)(2,1)} %param.19) | copy-start | bytes 6291460
  6.5 66.7 %all-gather.5.cloned.1.call-start = ((), (), s32[]{:S(2)}) async-start(), calls=%async_computation.6 | async-start | bytes 2228224 | tf_op jit(solution)/shard_map/all_gather | solution.py:81
  8.3 137.2 %all-gather.3.cloned.1.call-start = ((), (), s32[]{:S(2)}) async-start(), calls=%async_computation.5 | async-start | bytes 8912896 | tf_op jit(solution)/shard_map/all_gather | solution.py:80
  13.0 7.3 %copy-start.7 = (bf16[1024]{0:T(1024)(128)(2,1)S(1)}, bf16[1024]{0:T(1024)(128)(2,1)}, u32[]{:S(2)}) copy-start(bf16[1024]{0:T(1024)(128)(2,1)} %param.14) | copy-start | bytes 6148
  13.0 7.3 %copy-start.4 = (bf16[512,1024]{1,0:T(8,128)(2,1)S(1)}, bf16[512,1024]{1,0:T(8,128)(2,1)}, u32[]{:S(2)}) copy-start(bf16[512,1024]{1,0:T(8,128)(2,1)} %param.13) | copy-start | bytes 3145732
  13.0 41.2 %all-to-all-start = ((bf16[16,64,8,128]{3,2,1,0:T(8,128)(2,1)}), bf16[16,64,8,128]{3,2,1,0:T(8,128)(2,1)}, u32[]{:S(2)}, u32[]{:S(2)}) async-start(bf16[16,64,8,128]{3,2,1,0:T(8,128)(2,1)} %stack.2), calls=%async_computation | async-start | bytes 4194304 | tf_op jit(solution)/shard_map/all_to_all | solution.py:11
  20.2 222.1 %reduce-scatter.2.cloned.1.call-start = ((), (), s32[]{:S(2)}) async-start(), calls=%async_computation.7 | async-start | bytes 14155776 | tf_op jit(solution)/shard_map/reduce_scatter | solution.py:91
  145.5 7.5 %copy-start.2 = (f32[512,1024]{0,1:S(1)}, f32[512,1024]{0,1}, u32[]{:S(2)}) copy-start(f32[512,1024]{0,1} %fusion.60) | copy-start | bytes 6291460
  145.5 7.5 %copy-start.3 = (f32[8,512,128]{1,2,0:T(8,128)S(1)}, f32[8,512,128]{1,2,0:T(8,128)}, u32[]{:S(2)}) copy-start(f32[8,512,128]{1,2,0:T(8,128)} %convolution_bitcast_fusion.1) | copy-start | bytes 6291460
  172.5 0.7 copy-start.6
  172.5 11.9 %copy-start.8 = (s32[1,32]{1,0:T(1,128)S(1)}, s32[1,32]{1,0:T(1,128)}, u32[]{:S(2)}) copy-start(s32[1,32]{1,0:T(1,128)} %param.21) | copy-start | bytes 388
  179.1 67.8 %all-to-all-start.2 = ((bf16[16,1,64]{2,1,0:T(2,128)(2,1)}), bf16[16,1,64]{2,1,0:T(2,128)(2,1)S(1)}, u32[]{:S(2)}, u32[]{:S(2)}) async-start(bf16[16,1,64]{2,1,0:T(2,128)(2,1)} %all_to_all.20), calls=%async_computation.3 | async-start | bytes 16384 | tf_op jit(solution)/shard_map/all_to_all | solution.py:115
  246.9 35.1 %all-to-all-start.1 = ((bf16[16,64,768]{2,1,0:T(8,128)(2,1)}), bf16[16,64,768]{2,1,0:T(8,128)(2,1)}, u32[]{:S(2)}, u32[]{:S(2)}) async-start(bf16[16,64,768]{2,1,0:T(8,128)(2,1)} %bitcast.20), calls=%async_computation.2 | async-start | bytes 3145728 | tf_op jit(solution)/shard_map/all_to_all | solution.py:108
  299.6 1.5 copy-start.5
  306.7 1.5 copy-start.5
  313.9 1.5 copy-start.5
  321.0 1.5 copy-start.5
  328.1 1.5 copy-start.5
  335.2 1.5 copy-start.5
  342.4 1.5 copy-start.5
  349.5 1.5 copy-start.5
  354.7 21.9 %all-to-all-start.3 = ((bf16[16,64,512]{2,1,0:T(8,128)(2,1)}), bf16[16,64,512]{2,1,0:T(8,128)(2,1)S(1)}, u32[]{:S(2)}, u32[]{:S(2)}) async-start(bf16[16,64,512]{2,1,0:T(8,128)(2,1)} %reshape.284), calls=%async_computation.4 | async-start | bytes 2097152 | tf_op jit(solution)/shard_map/all_to_all | solution.py:162
  376.6 2.6 copy-start.1
Sparse Core Ops, SparseCore 0:
  9.5 63.7 all-gather.4
  75.4 70.0 all-gather.2
  172.6 69.6 reduce-scatter.1
